TPU v7x, 512 devices: a whole 4x4x16 slice. The times are simulated.
512 devices in a mesh: rep: 4 (over z_hi), exp: 16 (over x, y), mdl: 8 (over z_lo, core).
Axes of the slice: x: 4, y: 4, z: 16 (z_hi: 4, z_lo: 4; z = z_hi * 4 + z_lo), core: 2. Of those that a mesh axis runs over, the one named last changes fastest.
Arguments:
- inner_experts: bfloat16 [4, 16, 2, 768, 2048], P('rep', 'exp', None, None, 'mdl'), may hold values from -6 to 6
- inner_dense: bfloat16 [4, 9216, 768], P('rep', ('exp', 'mdl')), may hold values from -6 to 6
- inner_small: bfloat16 [4, 18, 768], P('rep'), may hold values from -6 to 6
- inner_embed: bfloat16 [4, 8192, 768], P('rep', ('exp', 'mdl')), may hold values from -6 to 6
- outer_experts: float32 [16, 2, 768, 2048], P('exp', None, ('rep', 'mdl')), may hold values from -6 to 6
- outer_dense: float32 [9216, 768], P(('exp', 'mdl'), 'rep'), may hold values from -6 to 6
- outer_small: float32 [18, 768], P(None, 'rep'), may hold values from -6 to 6
- outer_embed: float32 [8192, 768], P(('exp', 'mdl'), 'rep'), may hold values from -6 to 6
- moment_experts: float32 [16, 2, 768, 2048], P('exp', None, ('rep', 'mdl')), may hold values from -3 to 3
- moment_dense: float32 [9216, 768], P(('exp', 'mdl'), 'rep'), may hold values from -3 to 3
- moment_small: float32 [18, 768], P(None, 'rep'), may hold values from -3 to 3
- moment_embed: float32 [8192, 768], P(('exp', 'mdl'), 'rep'), may hold values from -3 to 3
- embed_basis: float32 [768, 64], replicated, may hold values from -0.21875 to 0.21875
Outputs:
- new_outer_experts: float32 [16, 2, 768, 2048], P('exp', None, ('rep', 'mdl'))
- new_moment_experts: float32 [16, 2, 768, 2048], P('exp', None, ('rep', 'mdl'))
- copy_experts: bfloat16 [16, 2, 768, 2048], P('exp', None, None, 'mdl')
- new_outer_dense: float32 [9216, 768], P(('exp', 'mdl'), 'rep')
- new_moment_dense: float32 [9216, 768], P(('exp', 'mdl'), 'rep')
- copy_dense: bfloat16 [9216, 768], P(('exp', 'mdl'))
- new_outer_small: float32 [18, 768], P(None, 'rep')
- new_moment_small: float32 [18, 768], P(None, 'rep')
- copy_small: bfloat16 [18, 768], replicated
- new_outer_embed: float32 [8192, 768], P(('exp', 'mdl'), 'rep')
- new_moment_embed: float32 [8192, 768], P(('exp', 'mdl'), 'rep')
- copy_embed: bfloat16 [8192, 768], P(('exp', 'mdl'))
All inputs are finite; a program needn't handle non-finite values.
Results may differ from a plain program's by a relative error of at most 0.012.
Values may be sent and summed in bfloat16 or wider, within the bound.
No kernel may reach another device: no remote copies, remote signals or barrier semaphores. Data moves between devices by JAX's collectives and lax.ppermute only.
A program may use at most 64 MiB of HBM per device.

v0:
```python
import jax
import jax.numpy as jnp
from jax import lax
from jax.sharding import PartitionSpec as P

decay_rate = 0.5
outer_rate = 0.7


def nesterov(outer, moment, grad_value):
    moment_new = decay_rate * moment + grad_value
    outer_new = outer - outer_rate * (grad_value + decay_rate * moment_new)
    return (outer_new, moment_new)


def on_device(
    inner_experts,
    inner_dense,
    inner_small,
    inner_embed,
    outer_experts,
    outer_dense,
    outer_small,
    outer_embed,
    moment_experts,
    moment_dense,
    moment_small,
    moment_embed,
    embed_basis,
):
    groups = lax.axis_size("rep")
    own_shard = inner_experts[0, 0]
    row_count = outer_experts.shape[2]
    full_width = outer_experts.shape[3]
    pieces = lax.all_to_all(own_shard, ("rep", "mdl"), split_axis=1, concat_axis=2, tiled=True)
    expert_sum = jnp.sum(
        pieces.reshape(2, row_count, groups, full_width), axis=2, dtype=jnp.float32
    )
    grad_experts = outer_experts[0] - expert_sum / groups
    dense_sum, small_sum = (
        lax.psum_scatter(
            inner_dense[0].astype(jnp.float32).astype(jnp.bfloat16),
            "rep",
            scatter_dimension=1,
            tiled=True,
        ).astype(jnp.float32),
        lax.psum_scatter(
            inner_small[0].astype(jnp.float32).astype(jnp.bfloat16),
            "rep",
            scatter_dimension=1,
            tiled=True,
        ).astype(jnp.float32),
    )
    grad_dense = outer_dense - dense_sum / groups
    grad_small = outer_small - small_sum / groups
    col_count = outer_embed.shape[1]
    offset = lax.axis_index("rep") * col_count
    basis_part = lax.dynamic_slice_in_dim(embed_basis, offset, col_count, 0)
    partial_value = jnp.dot(
        outer_embed, basis_part, precision=lax.Precision.HIGHEST, preferred_element_type=jnp.float32
    )
    partial_value = (
        partial_value
        - jnp.dot(
            inner_embed[0].astype(jnp.float32),
            embed_basis,
            precision=lax.Precision.HIGHEST,
            preferred_element_type=jnp.float32,
        )
        / groups
    )
    coefficient = lax.psum(partial_value, "rep")
    grad_embed = jnp.dot(
        coefficient,
        basis_part.T,
        precision=lax.Precision.HIGHEST,
        preferred_element_type=jnp.float32,
    )
    expert_outer, expert_moment = nesterov(outer_experts[0], moment_experts[0], grad_experts)
    dense_outer, dense_moment = nesterov(outer_dense, moment_dense, grad_dense)
    small_outer, small_moment = nesterov(outer_small, moment_small, grad_small)
    embed_outer, embed_moment = nesterov(outer_embed, moment_embed, grad_embed)
    spread = lax.all_to_all(
        expert_outer.astype(jnp.bfloat16), "mdl", split_axis=2, concat_axis=1, tiled=True
    )
    copies = (
        lax.all_gather(spread, "rep", axis=1, tiled=True),
        lax.all_gather(dense_outer.astype(jnp.bfloat16), "rep", axis=1, tiled=True),
        lax.all_gather(small_outer.astype(jnp.bfloat16), "rep", axis=1, tiled=True),
        lax.all_gather(embed_outer.astype(jnp.bfloat16), "rep", axis=1, tiled=True),
    )
    return (
        expert_outer[None],
        expert_moment[None],
        copies[0][None],
        dense_outer,
        dense_moment,
        copies[1],
        small_outer,
        small_moment,
        copies[2],
        embed_outer,
        embed_moment,
        copies[3],
    )


def solution(mesh):
    placed = (
        P("rep", "exp", None, None, "mdl"),
        P("rep", ("exp", "mdl"), None),
        P("rep", None, None),
        P("rep", ("exp", "mdl"), None),
        P("exp", None, ("rep", "mdl"), None),
        P(("exp", "mdl"), "rep"),
        P(None, "rep"),
        P(("exp", "mdl"), "rep"),
        P("exp", None, ("rep", "mdl"), None),
        P(("exp", "mdl"), "rep"),
        P(None, "rep"),
        P(("exp", "mdl"), "rep"),
        P(),
    )
    return jax.shard_map(
        on_device,
        mesh=mesh,
        in_specs=placed,
        out_specs=(
            P("exp", None, ("rep", "mdl"), None),
            P("exp", None, ("rep", "mdl"), None),
            P("exp", None, None, "mdl"),
            P(("exp", "mdl"), "rep"),
            P(("exp", "mdl"), "rep"),
            P(("exp", "mdl"), None),
            P(None, "rep"),
            P(None, "rep"),
            P(),
            P(("exp", "mdl"), "rep"),
            P(("exp", "mdl"), "rep"),
            P(("exp", "mdl"), None),
        ),
        check_vma=False,
    )
```

profile of v0, /device:TPU:68, one launch (start us, length us, event | category | flops | bytes accessed | tf_op | source)
XLA Modules:
  0.0 202.1 jit_solution(756205942519219298)
XLA Ops:
  7.2 0.0 copy-start
  7.2 0.0 copy-start.9
  7.2 0.0 copy-start.4
  7.2 2.9 %copy.73 = bf16[1,1,2,768,256]{4,2,3,1,0:T(2,128)(2,1)} copy(bf16[1,1,2,768,256]{4,3,2,1,0:T(8,128)(2,1)} %param.13) | data formatting | bytes 1572864 | tf_op args[0]
  10.1 0.0 copy-start.3
  10.1 0.0 copy-start.5
  10.1 0.0 copy-start.8
  10.1 15.0 %all-to-all-start = ((bf16[2,768,256]{2,0,1:T(2,128)(2,1)}), bf16[2,768,256]{2,0,1:T(2,128)(2,1)S(1)}, u32[]{:S(2)}, u32[]{:S(2)}) async-start(bf16[2,768,256]{2,0,1:T(2,128)(2,1)} %bitcast.75), calls=%async_computation | async-start | bytes 1572864 | tf_op jit(solution)/shard_map/all_to_all | solution.py:35
  25.1 0.0 copy-start.10
  25.1 0.0 copy-start.11
  25.2 0.0 reduce-scatter.9.cloned.1.call-start
  25.2 0.0 copy-done.9
  25.2 0.8 copy.68
  26.0 0.0 reduce-scatter.9.cloned.1.call-update
  26.1 0.0 reduce-scatter.7.cloned.1.call-start
  26.1 0.0 copy-done.4
  26.1 0.8 copy.66
  26.9 0.0 reduce-scatter.7.cloned.1.call-update
  27.0 0.0 copy-done
  27.0 0.0 copy-done.3
  27.0 0.3 convolution_bitcast_fusion
  27.3 0.0 copy-done.5
  27.3 0.2 fusion
  27.5 58.3 %psum.7 = f32[64,64]{0,1:T(8,128)S(1)} all-reduce(f32[64,64]{0,1:T(8,128)S(1)} %fusion), channel_id=1, replica_groups=mesh['rep'=4,'exp'=16,'mdl'=8] {'rep'}, use_global_device_ids=true, to_apply=%region_3.0 | all-reduce | flops 4096 | bytes 32768 | tf_op jit(solution)/shard_map/psum | solution.py:72
  85.8 0.0 copy-done.8
  85.8 1.0 convert_bitcast_fusion.1
  86.7 19.4 %all-gather.2 = bf16[4,192,64]{1,2,0:T(8,128)(2,1)S(1)} all-gather(bf16[1,192,64]{1,2,0:T(8,128)(2,1)S(1)} %get-tuple-element.36), channel_id=1, replica_groups=mesh['rep'=4,'exp'=16,'mdl'=8] {'rep'}, dimensions={0}, use_global_device_ids=true | all-gather | bytes 122880 | tf_op jit(solution)/shard_map/all_gather | solution.py:90
  106.2 0.1 copy.64
  106.3 0.8 reshape.49
  107.0 0.0 reduce-scatter.9.cloned.1.call-done
  107.0 0.9 copy.69
  107.9 0.0 copy-done.10
  107.9 0.0 copy-done.11
  107.9 0.6 convert_bitcast_fusion.2
  108.6 17.3 %all-gather.1 = bf16[4,192,18]{1,2,0:T(8,128)(2,1)S(1)} all-gather(bf16[1,192,18]{1,2,0:T(8,128)(2,1)S(1)} %get-tuple-element.39), channel_id=1, replica_groups=mesh['rep'=4,'exp'=16,'mdl'=8] {'rep'}, dimensions={0}, use_global_device_ids=true | all-gather | bytes 34560 | tf_op jit(solution)/shard_map/all_gather | solution.py:89
  125.9 0.7 reshape.47
  126.6 0.0 reduce-scatter.7.cloned.1.call-done
  126.6 0.9 copy.67
  127.5 0.0 all-to-all-done
  127.5 0.3 copy.72
  127.8 0.7 reshape.42
  128.5 0.0 copy-start.1
  128.5 0.0 copy-start.2
  128.5 1.0 reduce_sum.9
  129.5 0.0 copy-done.1
  129.5 0.1 copy-done.2
  129.6 0.1 fusion.5
  129.8 0.0 copy-start.6
  129.8 0.0 copy-start.7
  129.8 0.7 copy.59
  130.5 2.0 reshape.54
  132.5 7.1 %all-to-all-start.1 = ((bf16[8,2,6144]{2,1,0:T(2,128)(2,1)}), bf16[8,2,6144]{2,1,0:T(2,128)(2,1)S(1)}, u32[]{:S(2)}, u32[]{:S(2)}) async-start(bf16[8,2,6144]{2,1,0:T(2,128)(2,1)} %reshape.54), calls=%async_computation.1 | async-start | bytes 393216 | tf_op jit(solution)/shard_map/all_to_all | solution.py:83
  139.6 0.0 copy-done.6
  139.6 0.0 copy-done.7
  139.6 0.7 convert_bitcast_fusion
  140.3 17.7 %all-gather = bf16[4,192,72]{1,2,0:T(8,128)(2,1)S(1)} all-gather(bf16[1,192,72]{1,2,0:T(8,128)(2,1)S(1)} %get-tuple-element.42), channel_id=1, replica_groups=mesh['rep'=4,'exp'=16,'mdl'=8] {'rep'}, dimensions={0}, use_global_device_ids=true | all-gather | bytes 138240 | tf_op jit(solution)/shard_map/all_gather | solution.py:88
  158.0 0.1 copy.61
  158.1 0.8 reshape.45
  158.9 1.0 multiply_subtract_fusion
  159.9 0.0 all-to-all-done.1
  159.9 1.5 reshape.55
  161.4 0.6 copy.60
  162.0 32.3 %all_gather.12 = bf16[2,768,256]{2,1,0:T(8,128)(2,1)S(1)} all-gather(bf16[2,192,256]{2,1,0:T(8,128)(2,1)S(1)} %bitcast.83), channel_id=1, replica_groups=mesh['rep'=4,'exp'=16,'mdl'=8] {'rep'}, dimensions={1}, use_global_device_ids=true | all-gather | bytes 983040 | tf_op jit(solution)/shard_map/all_gather | solution.py:87
  194.4 0.9 copy.75
  (1 shorter events, 0.0 us)
Async XLA Ops:
  7.2 19.8 %copy-start = (f32[768,64]{0,1:T(8,128)S(1)}, f32[768,64]{0,1:T(8,128)}, u32[]{:S(2)}) copy-start(f32[768,64]{0,1:T(8,128)} %param.25) | copy-start | bytes 589828
  7.2 18.0 %copy-start.9 = (bf16[1,18,768]{2,1,0:T(8,128)(2,1)S(1)}, bf16[1,18,768]{2,1,0:T(8,128)(2,1)}, u32[]{:S(2)}) copy-start(bf16[1,18,768]{2,1,0:T(8,128)(2,1)} %param.15) | copy-start | bytes 82948
  7.2 18.9 %copy-start.4 = (bf16[1,72,768]{2,1,0:T(8,128)(2,1)S(1)}, bf16[1,72,768]{2,1,0:T(8,128)(2,1)}, u32[]{:S(2)}) copy-start(bf16[1,72,768]{2,1,0:T(8,128)(2,1)} %param.14) | copy-start | bytes 331780
  10.1 16.9 %copy-start.3 = (f32[64,192]{1,0:T(8,128)S(1)}, f32[64,192]{1,0:T(8,128)}, u32[]{:S(2)}) copy-start(f32[64,192]{1,0:T(8,128)} %param.20) | copy-start | bytes 147460
  10.1 17.2 %copy-start.5 = (bf16[1,64,768]{2,1,0:T(8,128)(2,1)S(1)}, bf16[1,64,768]{2,1,0:T(8,128)(2,1)}, u32[]{:S(2)}) copy-start(bf16[1,64,768]{2,1,0:T(8,128)(2,1)} %param.16) | copy-start | bytes 294916
  10.1 75.7 %copy-start.8 = (f32[64,192]{1,0:T(8,128)S(1)}, f32[64,192]{1,0:T(8,128)}, u32[]{:S(2)}) copy-start(f32[64,192]{1,0:T(8,128)} %param.24) | copy-start | bytes 147460
  10.1 117.4 %all-to-all-start = ((bf16[2,768,256]{2,0,1:T(2,128)(2,1)}), bf16[2,768,256]{2,0,1:T(2,128)(2,1)S(1)}, u32[]{:S(2)}, u32[]{:S(2)}) async-start(bf16[2,768,256]{2,0,1:T(2,128)(2,1)} %bitcast.75), calls=%async_computation | async-start | bytes 1572864 | tf_op jit(solution)/shard_map/all_to_all | solution.py:35
  25.1 82.8 %copy-start.10 = (f32[18,192]{1,0:T(8,128)S(1)}, f32[18,192]{1,0:T(8,128)}, u32[]{:S(2)}) copy-start(f32[18,192]{1,0:T(8,128)} %param.19) | copy-start | bytes 41476
  25.1 82.8 %copy-start.11 = (f32[18,192]{1,0:T(8,128)S(1)}, f32[18,192]{1,0:T(8,128)}, u32[]{:S(2)}) copy-start(f32[18,192]{1,0:T(8,128)} %param.23) | copy-start | bytes 41476
  25.2 81.9 %reduce-scatter.9.cloned.1.call-start = ((), (), s32[]{:S(2)}) async-start(), calls=%async_computation.5 | async-start | bytes 245760
  26.1 100.5 %reduce-scatter.7.cloned.1.call-start = ((), (), s32[]{:S(2)}) async-start(), calls=%async_computation.4 | async-start | bytes 245760
  128.5 1.0 copy-start.1
  128.5 1.1 copy-start.2
  129.8 9.9 %copy-start.6 = (f32[72,192]{1,0:T(8,128)S(1)}, f32[72,192]{1,0:T(8,128)}, u32[]{:S(2)}) copy-start(f32[72,192]{1,0:T(8,128)} %param.18) | copy-start | bytes 165892
  129.8 9.9 %copy-start.7 = (f32[72,192]{1,0:T(8,128)S(1)}, f32[72,192]{1,0:T(8,128)}, u32[]{:S(2)}) copy-start(f32[72,192]{1,0:T(8,128)} %param.22) | copy-start | bytes 165892
  132.5 27.4 %all-to-all-start.1 = ((bf16[8,2,6144]{2,1,0:T(2,128)(2,1)}), bf16[8,2,6144]{2,1,0:T(2,128)(2,1)S(1)}, u32[]{:S(2)}, u32[]{:S(2)}) async-start(bf16[8,2,6144]{2,1,0:T(2,128)(2,1)} %reshape.54), calls=%async_computation.1 | async-start | bytes 393216 | tf_op jit(solution)/shard_map/all_to_all | solution.py:83
Sparse Core Ops, SparseCore 0:
  29.3 40.5 reduce-scatter.8
  73.3 35.0 reduce-scatter.6
where the time goes:
time: 203 us; the launch traced here: 202 us
  blocking collectives  145 us (71%)
  starting transfers between devices  22.2 us (11%)
  local copies, waits for them, and re-layouts  15.6 us (8%)
  between operations  14.3 us (7%)
  other arithmetic  3.39 us (2%)
    psum x1, blocking collectives, on_device(): coefficient = lax.psum(partial_value, 'rep')  58.3 us
    all_gather x1, blocking collectives, on_device(): lax.all_gather(spread, 'rep', axis=1, tiled=True)  32.3 us
    all_gather x1, blocking collectives, on_device(): lax.all_gather(embed_outer.astype(jnp.bfloat16), 'rep', axis=1, tiled=True)  19.4 us
    all_gather x1, blocking collectives, on_device(): lax.all_gather(dense_outer.astype(jnp.bfloat16), 'rep', axis=1, tiled=True)  17.7 us
    all_gather x1, blocking collectives, on_device(): lax.all_gather(small_outer.astype(jnp.bfloat16), 'rep', axis=1, tiled=True)  17.3 us
    all_to_all x1, starting transfers between devices, on_device(): lax.all_to_all(own_shard, ('rep', 'mdl'), split_axis=1, concat_axis=2, ti...  15 us
    unnamed x35, local copies, waits for them, and re-layouts  13.1 us
    all_to_all x1, starting transfers between devices, on_device(): lax.all_to_all(expert_outer.astype(jnp.bfloat16), 'mdl', split_axis=2, co...  7.09 us
  transfers between devices with their start and end apart: 4, of which 0 were waited for; matrix products, arithmetic and copies ran while one was open for 5% of the time, Pallas kernels for 0%

commit v1 on v0

--- a/solution.py
+++ b/solution.py
@@ -5,6 +5,14 @@
 
 decay_rate = 0.5
 outer_rate = 0.7
+
+
+def supply_group_now(shard_in, bus_axis, ndim_at):
+    response = jnp.concatenate(
+        lax.all_to_all(jnp.stack([shard_in] * lax.axis_size(bus_axis)), bus_axis, 0, 0),
+        axis=ndim_at,
+    )
+    return response
 
 
 def nesterov(outer, moment, grad_value):
@@ -87,7 +95,7 @@
         lax.all_gather(spread, "rep", axis=1, tiled=True),
         lax.all_gather(dense_outer.astype(jnp.bfloat16), "rep", axis=1, tiled=True),
         lax.all_gather(small_outer.astype(jnp.bfloat16), "rep", axis=1, tiled=True),
-        lax.all_gather(embed_outer.astype(jnp.bfloat16), "rep", axis=1, tiled=True),
+        supply_group_now(embed_outer.astype(jnp.bfloat16), "rep", 1),
     )
     return (
         expert_outer[None],

time: 203 us -> 200 us (0.985)
  the two profiles are of different devices: /device:TPU:68 before, /device:TPU:92 now
where the time goes in v1:
time: 200 us
  blocking collectives  128 us (64%)
  starting transfers between devices  28.2 us (14%)
  local copies, waits for them, and re-layouts  16.3 us (8%)
  between operations  14.3 us (7%)
  waiting for transfers between devices  8.2 us (4%)
  other arithmetic  3.39 us (2%)
    psum x1, blocking collectives, on_device(): coefficient = lax.psum(partial_value, 'rep')  59.2 us
    all_gather x1, blocking collectives, on_device(): lax.all_gather(spread, 'rep', axis=1, tiled=True)  32.9 us
    all_gather x1, blocking collectives, on_device(): lax.all_gather(dense_outer.astype(jnp.bfloat16), 'rep', axis=1, tiled=True)  17.8 us
    all_gather x1, blocking collectives, on_device(): lax.all_gather(small_outer.astype(jnp.bfloat16), 'rep', axis=1, tiled=True)  17.8 us
    all_to_all x1, starting transfers between devices, on_device(): lax.all_to_all(own_shard, ('rep', 'mdl'), split_axis=1, concat_axis=2, ti...  15 us
    unnamed x34, local copies, waits for them, and re-layouts  12.3 us
    all_to_all x1, waiting for transfers between devices, supply_group_now(): lax.all_to_all(jnp.stack([shard_in] * lax.axis_size(bus_axis)), bus_axis,...  8.16 us
    all_to_all x1, starting transfers between devices, supply_group_now(): lax.all_to_all(jnp.stack([shard_in] * lax.axis_size(bus_axis)), bus_axis,...  6.58 us
  transfers between devices with their start and end apart: 5, of which 1 were waited for; matrix products, arithmetic and copies ran while one was open for 7% of the time, Pallas kernels for 0%

profile of v1, /device:TPU:92, one launch (start us, length us, event | category | flops | bytes accessed | tf_op | source)
XLA Modules:
  0.0 199.6 jit_solution(8712636283003313583)
XLA Ops:
  7.2 0.0 copy-start
  7.2 0.0 copy-start.9
  7.2 0.0 copy-start.4
  7.2 2.9 %copy.71 = bf16[1,1,2,768,256]{4,2,3,1,0:T(2,128)(2,1)} copy(bf16[1,1,2,768,256]{4,3,2,1,0:T(8,128)(2,1)} %param.13) | data formatting | bytes 1572864 | tf_op args[0]
  10.1 0.0 copy-start.3
  10.1 0.0 copy-start.5
  10.1 0.0 copy-start.8
  10.1 0.0 copy-start.10
  10.1 0.0 copy-start.11
  10.1 15.0 %all-to-all-start = ((bf16[2,768,256]{2,0,1:T(2,128)(2,1)}), bf16[2,768,256]{2,0,1:T(2,128)(2,1)S(1)}, u32[]{:S(2)}, u32[]{:S(2)}) async-start(bf16[2,768,256]{2,0,1:T(2,128)(2,1)} %bitcast.69), calls=%async_computation | async-start | bytes 1572864 | tf_op jit(solution)/shard_map/all_to_all | solution.py:43
  25.2 0.0 reduce-scatter.9.cloned.1.call-start
  25.2 0.0 copy-done.9
  25.2 0.8 copy.66
  26.0 0.0 reduce-scatter.9.cloned.1.call-update
  26.1 0.0 reduce-scatter.7.cloned.1.call-start
  26.1 0.0 copy-done.4
  26.1 0.8 copy.64
  26.9 0.0 reduce-scatter.7.cloned.1.call-update
  27.0 0.0 copy-done
  27.0 0.0 copy-done.3
  27.0 0.3 convolution_bitcast_fusion
  27.3 0.0 copy-done.5
  27.3 0.2 fusion
  27.5 59.2 %psum.7 = f32[64,64]{0,1:T(8,128)S(1)} all-reduce(f32[64,64]{0,1:T(8,128)S(1)} %fusion), channel_id=1, replica_groups=mesh['rep'=4,'exp'=16,'mdl'=8] {'rep'}, use_global_device_ids=true, to_apply=%region_3.0 | all-reduce | flops 4096 | bytes 32768 | tf_op jit(solution)/shard_map/psum | solution.py:80
  86.7 0.0 copy-done.8
  86.7 1.0 fusion.12
  87.7 0.9 copy.67
  88.5 0.0 copy-done.10
  88.5 0.0 copy-done.11
  88.5 0.6 convert_bitcast_fusion.1
  89.2 17.8 %all-gather.1 = bf16[4,192,18]{1,2,0:T(8,128)(2,1)S(1)} all-gather(bf16[1,192,18]{1,2,0:T(8,128)(2,1)S(1)} %get-tuple-element.39), channel_id=1, replica_groups=mesh['rep'=4,'exp'=16,'mdl'=8] {'rep'}, dimensions={0}, use_global_device_ids=true | all-gather | bytes 34560 | tf_op jit(solution)/shard_map/all_gather | solution.py:97
  107.0 0.7 reshape.57
  107.7 0.9 copy.65
  108.6 0.0 all-to-all-done
  108.6 0.7 stack.2
  109.3 6.6 %all-to-all-start.2 = ((bf16[4,64,192]{2,1,0:T(8,128)(2,1)}), bf16[4,64,192]{2,1,0:T(8,128)(2,1)S(1)}, u32[]{:S(2)}, u32[]{:S(2)}) async-start(bf16[4,64,192]{2,1,0:T(8,128)(2,1)} %stack.2), calls=%async_computation.2 | async-start | bytes 262144 | tf_op jit(solution)/shard_map/all_to_all | solution.py:12
  115.9 0.3 copy.70
  116.1 0.7 reshape.52
  116.9 0.0 copy-start.1
  116.9 0.0 copy-start.2
  116.9 1.0 reduce_sum.9
  117.9 0.0 copy-done.1
  117.9 0.1 copy-done.2
  118.0 0.1 fusion.5
  118.1 0.0 copy-start.6
  118.1 0.0 copy-start.7
  118.2 0.7 copy.57
  118.9 2.0 %reshape.62 = bf16[8,2,6144]{2,1,0:T(2,128)(2,1)} reshape(bf16[2048,2,24]{2,1,0:T(2,128)(2,1)S(1)} %bitcast.71) | data formatting | bytes 393216
  120.9 8.2 %all-to-all-done.2 = bf16[4,64,192]{2,1,0:T(8,128)(2,1)S(1)} async-done(((bf16[4,64,192]{2,1,0:T(8,128)(2,1)}), bf16[4,64,192]{2,1,0:T(8,128)(2,1)S(1)}, u32[]{:S(2)}, u32[]{:S(2)}) %all-to-all-start.2) | async-done | bytes 98336 | tf_op jit(solution)/shard_map/all_to_all | solution.py:12
  129.1 6.5 %all-to-all-start.1 = ((bf16[8,2,6144]{2,1,0:T(2,128)(2,1)}), bf16[8,2,6144]{2,1,0:T(2,128)(2,1)S(1)}, u32[]{:S(2)}, u32[]{:S(2)}) async-start(bf16[8,2,6144]{2,1,0:T(2,128)(2,1)} %reshape.62), calls=%async_computation.1 | async-start | bytes 393216 | tf_op jit(solution)/shard_map/all_to_all | solution.py:91
  135.6 0.0 copy-done.6
  135.6 0.0 copy-done.7
  135.6 0.7 convert_bitcast_fusion
  136.3 17.8 %all-gather = bf16[4,192,72]{1,2,0:T(8,128)(2,1)S(1)} all-gather(bf16[1,192,72]{1,2,0:T(8,128)(2,1)S(1)} %get-tuple-element.42), channel_id=1, replica_groups=mesh['rep'=4,'exp'=16,'mdl'=8] {'rep'}, dimensions={0}, use_global_device_ids=true | all-gather | bytes 138240 | tf_op jit(solution)/shard_map/all_gather | solution.py:96
  154.1 0.1 copy.59
  154.2 0.8 reshape.55
  155.0 0.1 copy.62
  155.1 0.8 reshape.51
  155.8 1.0 multiply_subtract_fusion
  156.8 0.0 all-to-all-done.1
  156.8 1.5 reshape.63
  158.3 0.6 copy.58
  158.9 32.9 %all_gather.9 = bf16[2,768,256]{2,1,0:T(8,128)(2,1)S(1)} all-gather(bf16[2,192,256]{2,1,0:T(8,128)(2,1)S(1)} %bitcast.77), channel_id=1, replica_groups=mesh['rep'=4,'exp'=16,'mdl'=8] {'rep'}, dimensions={1}, use_global_device_ids=true | all-gather | bytes 983040 | tf_op jit(solution)/shard_map/all_gather | solution.py:95
  191.9 0.9 copy.73
  (3 shorter events, 0.0 us)
Async XLA Ops:
  7.2 19.8 %copy-start = (f32[768,64]{0,1:T(8,128)S(1)}, f32[768,64]{0,1:T(8,128)}, u32[]{:S(2)}) copy-start(f32[768,64]{0,1:T(8,128)} %param.25) | copy-start | bytes 589828
  7.2 18.0 %copy-start.9 = (bf16[1,18,768]{2,1,0:T(8,128)(2,1)S(1)}, bf16[1,18,768]{2,1,0:T(8,128)(2,1)}, u32[]{:S(2)}) copy-start(bf16[1,18,768]{2,1,0:T(8,128)(2,1)} %param.15) | copy-start | bytes 82948
  7.2 18.9 %copy-start.4 = (bf16[1,72,768]{2,1,0:T(8,128)(2,1)S(1)}, bf16[1,72,768]{2,1,0:T(8,128)(2,1)}, u32[]{:S(2)}) copy-start(bf16[1,72,768]{2,1,0:T(8,128)(2,1)} %param.14) | copy-start | bytes 331780
  10.1 16.9 %copy-start.3 = (f32[64,192]{1,0:T(8,128)S(1)}, f32[64,192]{1,0:T(8,128)}, u32[]{:S(2)}) copy-start(f32[64,192]{1,0:T(8,128)} %param.20) | copy-start | bytes 147460
  10.1 17.2 %copy-start.5 = (bf16[1,64,768]{2,1,0:T(8,128)(2,1)S(1)}, bf16[1,64,768]{2,1,0:T(8,128)(2,1)}, u32[]{:S(2)}) copy-start(bf16[1,64,768]{2,1,0:T(8,128)(2,1)} %param.16) | copy-start | bytes 294916
  10.1 76.6 %copy-start.8 = (f32[64,192]{1,0:T(8,128)S(1)}, f32[64,192]{1,0:T(8,128)}, u32[]{:S(2)}) copy-start(f32[64,192]{1,0:T(8,128)} %param.24) | copy-start | bytes 147460
  10.1 78.4 %copy-start.10 = (f32[18,192]{1,0:T(8,128)S(1)}, f32[18,192]{1,0:T(8,128)}, u32[]{:S(2)}) copy-start(f32[18,192]{1,0:T(8,128)} %param.19) | copy-start | bytes 41476
  10.1 78.4 %copy-start.11 = (f32[18,192]{1,0:T(8,128)S(1)}, f32[18,192]{1,0:T(8,128)}, u32[]{:S(2)}) copy-start(f32[18,192]{1,0:T(8,128)} %param.23) | copy-start | bytes 41476
  10.1 98.5 %all-to-all-start = ((bf16[2,768,256]{2,0,1:T(2,128)(2,1)}), bf16[2,768,256]{2,0,1:T(2,128)(2,1)S(1)}, u32[]{:S(2)}, u32[]{:S(2)}) async-start(bf16[2,768,256]{2,0,1:T(2,128)(2,1)} %bitcast.69), calls=%async_computation | async-start | bytes 1572864 | tf_op jit(solution)/shard_map/all_to_all | solution.py:43
  25.2 62.5 %reduce-scatter.9.cloned.1.call-start = ((), (), s32[]{:S(2)}) async-start(), calls=%async_computation.6 | async-start | bytes 245760
  26.1 81.7 %reduce-scatter.7.cloned.1.call-start = ((), (), s32[]{:S(2)}) async-start(), calls=%async_computation.5 | async-start | bytes 245760
  109.3 19.8 %all-to-all-start.2 = ((bf16[4,64,192]{2,1,0:T(8,128)(2,1)}), bf16[4,64,192]{2,1,0:T(8,128)(2,1)S(1)}, u32[]{:S(2)}, u32[]{:S(2)}) async-start(bf16[4,64,192]{2,1,0:T(8,128)(2,1)} %stack.2), calls=%async_computation.2 | async-start | bytes 262144 | tf_op jit(solution)/shard_map/all_to_all | solution.py:12
  116.9 1.0 copy-start.1
  116.9 1.1 copy-start.2
  118.1 17.4 %copy-start.6 = (f32[72,192]{1,0:T(8,128)S(1)}, f32[72,192]{1,0:T(8,128)}, u32[]{:S(2)}) copy-start(f32[72,192]{1,0:T(8,128)} %param.18) | copy-start | bytes 165892
  118.1 17.4 %copy-start.7 = (f32[72,192]{1,0:T(8,128)S(1)}, f32[72,192]{1,0:T(8,128)}, u32[]{:S(2)}) copy-start(f32[72,192]{1,0:T(8,128)} %param.22) | copy-start | bytes 165892
  129.1 27.8 %all-to-all-start.1 = ((bf16[8,2,6144]{2,1,0:T(2,128)(2,1)}), bf16[8,2,6144]{2,1,0:T(2,128)(2,1)S(1)}, u32[]{:S(2)}, u32[]{:S(2)}) async-start(bf16[8,2,6144]{2,1,0:T(2,128)(2,1)} %reshape.62), calls=%async_computation.1 | async-start | bytes 393216 | tf_op jit(solution)/shard_map/all_to_all | solution.py:91
Sparse Core Ops, SparseCore 0:
  29.3 40.9 reduce-scatter.8
  73.7 33.4 reduce-scatter.6
